TPU v7x, 128 devices: a whole 4x4x4 slice. The times are simulated.
128 devices in a mesh: replica: 8 (over z_lo, y), space: 16 (over z_hi, x, core).
Axes of the slice: x: 4, y: 4, z: 4 (z_hi: 2, z_lo: 2; z = z_hi * 2 + z_lo), core: 2. Of those that a mesh axis runs over, the one named last changes fastest.
Arguments:
- inputs: bfloat16 [8, 128, 512, 256], P('replica', 'space'), may hold values from -6 to 6
- cotangent: bfloat16 [8, 128, 512, 256], P('replica', 'space'), may hold values from -6 to 6
- land_mask: int32 [128, 512], P('space'), may hold values 0 or 1
- weights: float32 [8, 2, 2304, 256], P('replica', None, 'space'), may hold values from -0.125 to 0.125
- momentum: float32 [8, 2, 2304, 256], P('replica', None, 'space'), may hold values from -6 to 6
- step: int32 [1], replicated, may hold values from 0 to 63
Outputs:
- grad_input: bfloat16 [8, 128, 512, 256], P('replica', 'space')
- new_weights: float32 [8, 2, 2304, 256], P('replica', None, 'space')
- new_momentum: float32 [8, 2, 2304, 256], P('replica', None, 'space')
All inputs are finite; a program needn't handle non-finite values. No bound on the sum of `land_mask` on one device may be relied on, other than what follows from the above.
Results may differ from a plain program's by a relative error of at most 0.012.
Values may be sent and summed in bfloat16 or wider, within the bound.
No kernel may reach another device: no remote copies, remote signals or barrier semaphores. Data moves between devices by JAX's collectives and lax.ppermute only.
A program may use at most 256 MiB of HBM per device.

v0:
```python
from functools import partial
import math

import jax
import jax.numpy as jnp
from jax import lax
from jax.sharding import PartitionSpec as P


def extended_2(shard, sides, width):
    for axis, dim in sides:
        size, length = (lax.axis_size(axis), shard.shape[dim])
        up = [(i, (i + 1) % size) for i in range(size - 1)]
        down = [(j, i) for i, j in up]
        last = lax.slice_in_dim(shard, length - width, length, axis=dim)
        initial = lax.slice_in_dim(shard, 0, width, axis=dim)
        before = lax.ppermute(last, axis, up)
        after = lax.ppermute(initial, axis, down)
        shard = jnp.concatenate([before, shard, after], axis=dim)
    return shard


def as_sent(shard):

    def short(part):
        return part.astype(jnp.bfloat16) if part.dtype == jnp.float32 else part

    return jax.tree.map(short, shard)


def passed_along(shard, axis, by):
    length = lax.axis_size(axis)
    return lax.ppermute(shard, axis, [(i, (i + by) % length) for i in range(length)])


def conv_ahead(extended, kernel):
    chan_count = extended.shape[-1]
    taps = kernel.reshape(3, 3, chan_count, kernel.shape[1])
    return lax.conv_general_dilated(
        extended[None],
        taps,
        (1, 1),
        ((0, 0), (1, 1)),
        dimension_numbers=("NHWC", "HWIO", "NHWC"),
        preferred_element_type=jnp.float32,
    )[0]


def conv_behind(extended, kernel):
    chan_count = kernel.shape[0] // 9
    taps = jnp.flip(kernel.reshape(3, 3, chan_count, kernel.shape[1]), (0, 1))
    return lax.conv_general_dilated(
        extended[None],
        taps,
        (1, 1),
        ((0, 0), (1, 1)),
        dimension_numbers=("NHWC", "HWOI", "NHWC"),
        preferred_element_type=jnp.float32,
    )[0]


def kernel_grad(extended, upstream):
    grad = lax.conv_general_dilated(
        extended[None],
        upstream[None],
        (1, 1),
        ((0, 0), (1, 1)),
        dimension_numbers=("CHWN", "IHWO", "HWNC"),
        preferred_element_type=jnp.float32,
    )
    return grad.reshape(-1, grad.shape[-1])


def silu_slope(preact):
    sigma = jax.nn.sigmoid(preact)
    return sigma * (1.0 + preact * (1.0 - sigma))


def rim(stacked):
    return extended_2(stacked, (("space", 1),), 1)


def send_both(distance, stacked):
    return jax.tree.map(
        lambda part, own: part.astype(own.dtype),
        passed_along(as_sent(stacked), "replica", distance),
        stacked,
    )


def gossip(step, stacked, sender):
    levels = lax.axis_size("replica").bit_length() - 1
    received = lax.switch(
        step[0] % levels, [partial(sender, 1 << power) for power in range(levels)], stacked
    )
    return 0.5 * (stacked + received)


def shards(inputs, cotangent, land_mask, weights, momentum, step):
    row_count = inputs.shape[1]
    col_count = inputs.shape[2]
    space_count = lax.axis_size("space")
    masked = cotangent[0] * land_mask.astype(jnp.bfloat16)[:, :, None]
    kernels = lax.all_gather(weights.astype(jnp.bfloat16), "space", axis=2, tiled=True)
    kernel_first = kernels[0, 0]
    kernel_second = kernels[0, 1]
    paired = rim(jnp.stack([inputs[0], masked]))
    preact = conv_ahead(paired[0], kernel_first)
    hidden = jax.nn.silu(preact).astype(jnp.bfloat16)
    hidden_ext = rim(hidden[None])[0]
    back_mid = (conv_behind(paired[1], kernel_second) * silu_slope(preact)).astype(jnp.bfloat16)
    back_ext = rim(back_mid[None])[0]
    input_ext = paired[0]
    grad_input = (conv_behind(back_ext, kernel_first) + masked.astype(jnp.float32)).astype(
        jnp.bfloat16
    )[None]
    scale = 1.0 / math.sqrt(row_count * space_count * col_count)
    grad_second_full = kernel_grad(hidden_ext, masked) * scale
    grad_first_full = kernel_grad(input_ext, back_mid) * scale
    shares = lax.psum_scatter(
        jnp.stack([grad_first_full, grad_second_full])[None].astype(jnp.bfloat16),
        "space",
        scatter_dimension=2,
        tiled=True,
    ).astype(jnp.float32)
    moment = 0.9 * momentum + shares
    updated = weights - 0.01 * moment
    mixed = gossip(step, jnp.stack([updated, moment]), send_both)
    new_weights = mixed[0]
    new_momentum = mixed[1]
    return (grad_input, new_weights, new_momentum)


def solution(mesh):
    in_specs = (
        P("replica", "space", None, None),
        P("replica", "space", None, None),
        P("space", None),
        P("replica", None, "space", None),
        P("replica", None, "space", None),
        P(),
    )
    out_specs = (
        P("replica", "space", None, None),
        P("replica", None, "space", None),
        P("replica", None, "space", None),
    )
    return jax.shard_map(shards, mesh=mesh, in_specs=in_specs, out_specs=out_specs, check_vma=False)
```

profile of v0, /device:TPU:2, one launch (start us, length us, event | category | flops | bytes accessed | tf_op | source)
XLA Modules:
  0.0 250.0 jit_solution(1926238018206280387)
XLA Ops:
  10.0 2.8 %copy.49 = bf16[1,8,512,256]{3,1,2,0:T(8,128)(2,1)S(1)} copy(bf16[1,8,512,256]{3,2,1,0:T(8,128)(2,1)} %param.9) | data formatting | bytes 4194304 | tf_op args[0]
  12.8 3.1 %copy_multiply_fusion = bf16[1,8,512,256]{3,1,2,0:T(8,128)(2,1)S(1)} fusion(bf16[1,8,512,256]{3,2,1,0:T(8,128)(2,1)S(1)} %copy-done.5, bf16[8,512]{0,1:T(8,128)(2,1)S(1)} %copy.47), kind=kLoop, calls=%fused_computation.58 | loop fusion | flops 1048576 | bytes 4202496 | tf_op jit(solution)/shard_map/mul | solution.py:103
  19.6 2.4 collective-permute-start.3
  22.0 5.0 %collective-permute-done.4 = bf16[2,1,512,256]{3,2,1,0:T(8,128)(2,1)S(1)} collective-permute-done((bf16[2,1,512,256]{3,2,1,0:T(8,128)(2,1)S(1)}, bf16[2,1,512,256]{3,2,1,0:T(8,128)(2,1)S(1)}, u32[]{:S(2)}, u32[]{:S(2)}) %collective-permute-start.4) | collective-permute-done | bytes 524320 | tf_op jit(solution)/shard_map/ppermute | solution.py:18
  27.8 3.9 %collective-permute-done.3 = bf16[2,1,512,256]{3,2,1,0:T(8,128)(2,1)S(1)} collective-permute-done((bf16[2,1,512,256]{3,2,1,0:T(8,128)(2,1)S(1)}, bf16[2,1,512,256]{3,2,1,0:T(8,128)(2,1)S(1)}, u32[]{:S(2)}, u32[]{:S(2)}) %collective-permute-start.3) | collective-permute-done | bytes 524320 | tf_op jit(solution)/shard_map/ppermute | solution.py:17
  32.5 6.1 %pad_maximum_fusion = bf16[2,10,512,256]{3,1,2,0:T(8,128)(2,1)S(1)} fusion(bf16[2,1,512,256]{3,1,2,0:T(2,128)(2,1)S(1)} %copy.53, bf16[1,8,512,256]{3,1,2,0:T(8,128)(2,1)S(1)} %copy_multiply_fusion, bf16[1,8,512,256]{3,1,2,0:T(8,128)(2,1)S(1)} %copy.49, bf16[2,1,512,256]{3,1,2,0:T(2,128)(2,1)S(1)} %copy.52), kind=kLoop, calls=%fused_computation | loop fusion | flops 20971520 | bytes 10485760 | tf_op jit(solution)/shard_map/concatenate | solution.py:19
  38.6 2.3 slice_bitcast_fusion.2
  41.9 2.5 %pad.2 = bf16[10,1,520,256]{3,0,2,1:T(8,128)(2,1)} pad(bf16[10,1,512,256]{3,0,2,1:T(8,128)(2,1)S(1)} %get-tuple-element.23, bf16[]{:T(256)} %constant.32), padding=0_0x0_0x1_7x0_0 | pad | bytes 5283842 | tf_op jit(solution)/shard_map/slice | solution.py:108
  44.6 3.0 %reshape.90 = bf16[10,1,8,65,256]{4,3,2,0,1:T(8,128)(2,1)} reshape(bf16[10,1,520,256]{3,2,0,1:T(8,128)(2,1)S(1)} %pad.4.clone) | data formatting | bytes 5324800 | tf_op jit(solution)/shard_map/slice | solution.py:108
  47.6 3.2 %reshape.95 = bf16[10,8,65,256,1]{3,2,1,0,4:T(8,128)(2,1)} reshape(bf16[10,1,520,256]{3,2,0,1:T(8,128)(2,1)S(1)} %pad.4.clone) | data formatting | bytes 5324800 | tf_op jit(solution)/shard_map/slice | solution.py:108
  50.9 3.3 %copy.59 = bf16[10,1,8,65,256]{4,2,3,0,1:T(8,128)(2,1)S(1)} copy(bf16[10,1,8,65,256]{4,0,3,2,1:T(8,128)(2,1)} %bitcast.72) | data formatting | bytes 5324800 | tf_op jit(solution)/shard_map/conv_general_dilated | solution.py:39
  54.9 2.5 copy.56
  58.4 1.9 fusion.70
  63.9 2.1 copy.75
  66.0 2.6 %fusion.37 = (bf16[10,8,65,256,1]{3,1,4,2,0:T(8,128)(2,1)}, bf16[10,8,65,256,1]{3,1,4,2,0:T(8,128)(2,1)}) fusion(bf16[10,1,7,1,256]{4,2,3,0,1:T(8,128)(2,1)S(1)} %copy.97, bf16[10,1,8,64,256]{4,2,3,0,1:T(8,128)(2,1)S(1)} %copy.96, bf16[10,1,8,64,256]{4,2,3,0,1:T(8,128)(2,1)S(1)} %copy.95, bf16[10,1,7,1,256]{4,2,3,0,1:T(8,128)(2,1)S(1)} %copy.94), kind=kLoop, calls=%fused_computation.46 | loop fusion | flops 15974400 | bytes 10639360 | tf_op jit(solution)/shard_map/slice | solution.py:108
  68.6 2.8 %fusion.72 = (bf16[1,1,2304,256]{3,2,1,0:T(8,128)(2,1)}, bf16[1,1,2304,256]{3,2,1,0:T(8,128)(2,1)S(1)}) fusion(bf16[1,2,2304,256]{3,2,1,0:T(8,128)(2,1)} %all-gather.2.cloned.1.call-done), kind=kLoop, calls=%fused_computation.86 | loop fusion | bytes 4718592 | tf_op jit(solution)/shard_map/slice | solution.py:106
  71.4 7.1 %multiply_convert_fusion.1 = (bf16[8,8,65,256]{3,1,2,0:T(8,128)(2,1)S(1)}, f32[8,8,65,256]{3,1,2,0:T(8,128)}) fusion(pred[8,65]{0,1:T(8,128)(4,1)S(1)} %copy-done.18, bf16[3,3,256,256]{3,2,1,0:T(8,128)(2,1)S(1)} %bitcast.78, bf16[10,1,7,2,256]{4,2,3,0,1:T(8,128)(2,1)S(1)} %slice.71, bf16[10,1,8,65,256]{4,2,3,0,1:T(8,128)(2,1)S(1)} %copy.59), kind=kOutput, calls=%fused_computation.18 | convolution fusion | flops 4921958400 | bytes 10304008 | tf_op jit(solution)/shard_map/conv_general_dilated | solution.py:39
  83.4 11.2 %collective-permute-start.7 = (bf16[1,1,512,256]{3,0,2,1:T(2,128)(2,1)S(1)}, bf16[1,1,512,256]{3,0,2,1:T(2,128)(2,1)S(1)}, u32[]{:S(2)}, u32[]{:S(2)}) collective-permute-start(bf16[1,1,512,256]{3,0,2,1:T(2,128)(2,1)S(1)} %slice.85), channel_id=1, source_target_pairs={{0,1},{1,2},{2,3},{3,4},{4,5},{5,6},{6,7},{7,8},{8,9},{9,10},{10,1... | collective-permute-start | bytes 786440 | tf_op jit(solution)/shard_map/ppermute | solution.py:17
  94.6 9.8 %multiply_convert_fusion = bf16[8,8,65,256]{3,1,2,0:T(8,128)(2,1)S(1)} fusion(f32[8,8,65,256]{3,1,2,0:T(8,128)} %get-tuple-element.41, bf16[3,3,256,256]{3,2,1,0:T(8,128)(2,1)} %bitcast.80, bf16[10,1,7,2,256]{4,2,3,0,1:T(8,128)(2,1)S(1)} %slice.68, bf16[10,1,8,65,256]{4,2,3,0,1:T(8,128)(2,1)} %copy.56, pred[8,65]{0,1:T(8,128)(4,1)S(1)} %copy-done.18), kind=kOutput, calls=%fused_computation.17 | convolution fusion | flops 4927283200 | bytes 10304008 | tf_op jit(solution)/shard_map/conv_general_dilated | solution.py:52
  104.4 9.8 %multiply_convert_fusion.2 = bf16[3,3,256,256,1]{3,2,1,4,0:T(8,128)(2,1)} fusion(bf16[8,8,65,256]{3,1,2,0:T(8,128)(2,1)S(1)} %multiply_convert_fusion, pred[8,65]{0,1:T(8,128)(4,1)S(1)} %copy-done.18, bf16[10,8,65,256,1]{3,1,4,2,0:T(8,128)(2,1)S(1)} %copy-done.9, bf16[10,8,65,256,1]{3,1,4,2,0:T(8,128)(2,1)S(1)} %copy-done.8, ...), kind=kOutput, calls=%fused_computation.50 | convolution fusion | flops 4917567488 | bytes 11297288 | tf_op jit(solution)/shard_map/conv_general_dilated | solution.py:63
  114.3 3.2 %copy.83 = bf16[1,8,512,256]{3,0,2,1:T(2,128)(2,1)S(1)} copy(bf16[1,8,512,256]{3,1,2,0:T(8,128)(2,1)S(1)} %slice_bitcast_fusion.3) | data formatting | bytes 4194304 | tf_op jit(solution)/shard_map/convert_element_type | solution.py:109
  117.6 35.1 %multiply_convert_fusion.3 = bf16[3,3,256,256]{3,2,1,0:T(8,128)(2,1)S(1)} fusion(bf16[1,8,512,256]{3,1,2,0:T(8,128)(2,1)S(1)} %copy-done.2, bf16[1,1,512,256]{3,0,2,1:T(2,128)(2,1)} %collective-permute-done.8, bf16[1,8,512,256]{3,0,2,1:T(2,128)(2,1)S(1)} %copy.83, bf16[1,1,512,256]{3,0,2,1:T(2,128)(2,1)S(1)} %collective-permute-done.7), kind=kOutput, calls=%fused_computation.51 | convolution fusion | flops 4834590720 | bytes 5898240 | tf_op jit(solution)/shard_map/conv_general_dilated | solution.py:63
  155.0 2.0 copy.61
  159.7 3.1 %collective-permute-start.6 = (bf16[1,1,512,256]{3,1,2,0:T(2,128)(2,1)}, bf16[1,1,512,256]{3,1,2,0:T(2,128)(2,1)}, u32[]{:S(2)}, u32[]{:S(2)}) collective-permute-start(bf16[1,1,512,256]{3,1,2,0:T(2,128)(2,1)} %slice.77), channel_id=1, source_target_pairs={{1,0},{2,1},{3,2},{4,3},{5,4},{6,5},{7,6},{8,7},{9,8},{10,9},{11,1... | collective-permute-start | bytes 786440 | tf_op jit(solution)/shard_map/ppermute | solution.py:18
  163.0 2.1 collective-permute-start.5
  165.3 5.4 %collective-permute-done.5 = bf16[1,1,512,256]{3,2,1,0:T(8,128)(2,1)S(1)} collective-permute-done((bf16[1,1,512,256]{3,2,1,0:T(8,128)(2,1)S(1)}, bf16[1,1,512,256]{3,2,1,0:T(8,128)(2,1)S(1)}, u32[]{:S(2)}, u32[]{:S(2)}) %collective-permute-start.5) | collective-permute-done | bytes 262176 | tf_op jit(solution)/shard_map/ppermute | solution.py:17
  171.2 3.9 %maximum_bitcast_fusion = bf16[10,1,512,256]{3,0,2,1:T(8,128)(2,1)S(1)} fusion(bf16[1,1,512,256]{3,1,2,0:T(2,128)(2,1)} %collective-permute-done.6, bf16[1,8,512,256]{3,1,2,0:T(8,128)(2,1)S(1)} %slice_bitcast_fusion.4, bf16[1,1,512,256]{3,1,2,0:T(2,128)(2,1)S(1)} %copy.64), kind=kLoop, calls=%fused_computation.25 | loop fusion | flops 7864320 | bytes 5242880 | tf_op jit(solution)/shard_map/concatenate | solution.py:19
  176.9 5.5 %broadcast_select_fusion = f32[8,8,65,256]{3,1,2,0:T(8,128)S(1)} fusion(pred[8,65]{0,1:T(8,128)(4,1)S(1)} %copy-done.19, bf16[3,3,256,256]{3,2,1,0:T(8,128)(2,1)S(1)} %bitcast.79, bf16[10,1,7,2,256]{4,2,3,0,1:T(8,128)(2,1)S(1)} %slice.78, bf16[10,1,8,65,256]{4,2,3,0,1:T(8,128)(2,1)S(1)} %copy.67), kind=kOutput, calls=%fused_computation.54 | convolution fusion | flops 4916633600 | bytes 8174088 | tf_op jit(solution)/shard_map/conv_general_dilated | solution.py:52
  184.1 3.1 %fusion.13 = bf16[1,8,512,256]{3,1,2,0:T(8,128)(2,1)S(1)} fusion(f32[8,1,520,256]{3,0,2,1:T(8,128)S(1)} %bitcast.75, bf16[8,512]{0,1:T(8,128)(2,1)S(1)} %copy-done.12, bf16[1,8,512,256]{3,2,1,0:T(8,128)(2,1)S(1)} %copy-done.6), kind=kLoop, calls=%fused_computation.22 | loop fusion | flops 4194304 | bytes 8396800 | tf_op jit(solution)/shard_map/convert_element_type | solution.py:114
  189.0 44.9 %reduce-scatter.2.cloned.1.call-done = bf16[1,2,144,256]{3,2,1,0:T(8,128)(2,1)} async-done(((bf16[1,2,2304,256]{3,2,1,0:T(8,128)(2,1)}), bf16[1,2,144,256]{3,2,1,0:T(8,128)(2,1)}) %reduce-scatter.2.cloned.1.call-update) | async-done | bytes 147472 | tf_op jit(solution)/shard_map/reduce_scatter | solution.py:120
  234.9 7.2 %conditional.4 = (f32[2,1,2,144,256]{4,3,2,1,0:T(8,128)S(1)}) conditional(s32[]{:T(128)} %clamp.3, bf16[2,1,2,144,256]{4,3,2,1,0:T(8,128)(2,1)S(1)} %pad_maximum_fusion.8, bf16[2,1,2,144,256]{4,3,2,1,0:T(8,128)(2,1)S(1)} %pad_maximum_fusion.8, bf16[2,1,2,144,256]{4,3,2,1,0:T(8,128)(2,1)S(1)} %pad_maximum_fusion.8), branch_computations={%region_1.2_spmd, %region_2.3_spmd, %region_3.4_spmd} | conditional | flops 147456 | bytes 2064432
  235.7 6.3 %collective-permute-done.2 = bf16[2,1,2,144,256]{4,3,2,1,0:T(8,128)(2,1)S(1)} collective-permute-done((bf16[2,1,2,144,256]{4,3,2,1,0:T(8,128)(2,1)S(1)}, bf16[2,1,2,144,256]{4,3,2,1,0:T(8,128)(2,1)S(1)}, u32[]{:S(2)}, u32[]{:S(2)}) %collective-permute-start.2) | collective-permute-done | bytes 294944 | tf_op jit(solution)/shard_map/cond/branch_2_fun/ppermute | solution.py:33
  (98 shorter events, 32.3 us)
Async XLA Ops:
  7.2 5.6 %copy-start.5 = (bf16[1,8,512,256]{3,2,1,0:T(8,128)(2,1)S(1)}, bf16[1,8,512,256]{3,2,1,0:T(8,128)(2,1)}, u32[]{:S(2)}) copy-start(bf16[1,8,512,256]{3,2,1,0:T(8,128)(2,1)} %param.10) | copy-start | bytes 6291460
  7.2 61.4 %all-gather.2.cloned.1.call-start = ((), (), s32[]{:S(2)}) async-start(), calls=%async_computation.1 | async-start | bytes 2506752 | tf_op jit(solution)/shard_map/all_gather | solution.py:104
  9.0 224.9 %reduce-scatter.2.cloned.1.call-start = ((), (), s32[]{:S(2)}) async-start(), calls=%async_computation.2 | async-start | bytes 2506752 | tf_op jit(solution)/shard_map/reduce_scatter | solution.py:120
  10.0 5.9 %copy-start.11 = (bf16[8,512]{0,1:T(8,128)(2,1)}, bf16[8,512]{0,1:T(8,128)(2,1)S(1)}, u32[]{:S(2)}) copy-start(bf16[8,512]{0,1:T(8,128)(2,1)S(1)} %copy.47) | copy-start | bytes 24580
  15.9 16.6 %copy-start.1 = (bf16[1,8,512,256]{3,1,2,0:T(8,128)(2,1)}, bf16[1,8,512,256]{3,1,2,0:T(8,128)(2,1)S(1)}, u32[]{:S(2)}) copy-start(bf16[1,8,512,256]{3,1,2,0:T(8,128)(2,1)S(1)} %copy_multiply_fusion) | copy-start | bytes 6291460
  17.5 9.4 %collective-permute-start.4 = (bf16[2,1,512,256]{3,2,1,0:T(8,128)(2,1)S(1)}, bf16[2,1,512,256]{3,2,1,0:T(8,128)(2,1)S(1)}, u32[]{:S(2)}, u32[]{:S(2)}) collective-permute-start(bf16[2,1,512,256]{3,2,1,0:T(8,128)(2,1)S(1)} %copy.51), channel_id=1, source_target_pairs={{1,0},{2,1},{3,2},{4,3},{5,4},{6,5},{7,6},{8,7},{9,8},{10,9},{11,1... | collective-permute-start | bytes 1572872 | tf_op jit(solution)/shard_map/ppermute | solution.py:18
  19.6 12.1 %collective-permute-start.3 = (bf16[2,1,512,256]{3,2,1,0:T(8,128)(2,1)S(1)}, bf16[2,1,512,256]{3,2,1,0:T(8,128)(2,1)S(1)}, u32[]{:S(2)}, u32[]{:S(2)}) collective-permute-start(bf16[2,1,512,256]{3,2,1,0:T(8,128)(2,1)S(1)} %copy.50), channel_id=1, source_target_pairs={{0,1},{1,2},{2,3},{3,4},{4,5},{5,6},{6,7},{7,8},{8,9},{9,10},{10,1... | collective-permute-start | bytes 1572872 | tf_op jit(solution)/shard_map/ppermute | solution.py:17
  50.9 3.5 %copy-start.3 = (bf16[10,1,512,256]{3,0,2,1:T(8,128)(2,1)S(1)}, bf16[10,1,512,256]{3,0,2,1:T(8,128)(2,1)}, u32[]{:S(2)}) copy-start(bf16[10,1,512,256]{3,0,2,1:T(8,128)(2,1)} %get-tuple-element.22) | copy-start | bytes 7864324
  54.9 3.4 %copy-start = (bf16[10,1,8,65,256]{4,3,2,0,1:T(8,128)(2,1)S(1)}, bf16[10,1,8,65,256]{4,3,2,0,1:T(8,128)(2,1)}, u32[]{:S(2)}) copy-start(bf16[10,1,8,65,256]{4,3,2,0,1:T(8,128)(2,1)} %reshape.90) | copy-start | bytes 7987204
  62.0 1.9 copy-start.4
  68.6 2.9 %copy-start.18 = (pred[8,65]{0,1:T(8,128)(4,1)S(1)}, pred[8,65]{0,1:T(8,128)(4,1)}, u32[]{:S(2)}) copy-start(pred[8,65]{0,1:T(8,128)(4,1)} %constant.49) | copy-start | bytes 1564
  71.4 7.1 %copy-start.14 = (bf16[1,1,2304,256]{3,2,1,0:T(8,128)(2,1)}, bf16[1,1,2304,256]{3,2,1,0:T(8,128)(2,1)S(1)}, u32[]{:S(2)}) copy-start(bf16[1,1,2304,256]{3,2,1,0:T(8,128)(2,1)S(1)} %get-tuple-element.31) | copy-start | bytes 3538948
  80.6 36.9 %collective-permute-start.8 = (bf16[1,1,512,256]{3,0,2,1:T(2,128)(2,1)}, bf16[1,1,512,256]{3,0,2,1:T(2,128)(2,1)}, u32[]{:S(2)}, u32[]{:S(2)}) collective-permute-start(bf16[1,1,512,256]{3,0,2,1:T(2,128)(2,1)} %slice.88), channel_id=1, source_target_pairs={{1,0},{2,1},{3,2},{4,3},{5,4},{6,5},{7,6},{8,7},{9,8},{10,9},{11,1... | collective-permute-start | bytes 786440 | tf_op jit(solution)/shard_map/ppermute | solution.py:18
  83.4 34.2 %collective-permute-start.7 = (bf16[1,1,512,256]{3,0,2,1:T(2,128)(2,1)S(1)}, bf16[1,1,512,256]{3,0,2,1:T(2,128)(2,1)S(1)}, u32[]{:S(2)}, u32[]{:S(2)}) collective-permute-start(bf16[1,1,512,256]{3,0,2,1:T(2,128)(2,1)S(1)} %slice.85), channel_id=1, source_target_pairs={{0,1},{1,2},{2,3},{3,4},{4,5},{5,6},{6,7},{7,8},{8,9},{9,10},{10,1... | collective-permute-start | bytes 786440 | tf_op jit(solution)/shard_map/ppermute | solution.py:17
  94.5 9.8 %copy-start.8 = (bf16[10,8,65,256,1]{3,1,4,2,0:T(8,128)(2,1)S(1)}, bf16[10,8,65,256,1]{3,1,4,2,0:T(8,128)(2,1)}, u32[]{:S(2)}) copy-start(bf16[10,8,65,256,1]{3,1,4,2,0:T(8,128)(2,1)} %copy.75) | copy-start | bytes 7987204
  94.6 9.8 %copy-start.9 = (bf16[10,8,65,256,1]{3,1,4,2,0:T(8,128)(2,1)S(1)}, bf16[10,8,65,256,1]{3,1,4,2,0:T(8,128)(2,1)}, u32[]{:S(2)}) copy-start(bf16[10,8,65,256,1]{3,1,4,2,0:T(8,128)(2,1)} %get-tuple-element.42) | copy-start | bytes 7987204
  94.6 9.8 %copy-start.10 = (bf16[10,8,65,256,1]{3,1,4,2,0:T(8,128)(2,1)S(1)}, bf16[10,8,65,256,1]{3,1,4,2,0:T(8,128)(2,1)}, u32[]{:S(2)}) copy-start(bf16[10,8,65,256,1]{3,1,4,2,0:T(8,128)(2,1)} %get-tuple-element.43) | copy-start | bytes 7987204
  104.3 9.8 %copy-start.7 = (bf16[8,8,65,256]{3,1,2,0:T(8,128)(2,1)}, bf16[8,8,65,256]{3,1,2,0:T(8,128)(2,1)S(1)}, u32[]{:S(2)}) copy-start(bf16[8,8,65,256]{3,1,2,0:T(8,128)(2,1)S(1)} %multiply_convert_fusion) | copy-start | bytes 6389764
  114.3 3.3 %copy-start.2 = (bf16[1,8,512,256]{3,1,2,0:T(8,128)(2,1)S(1)}, bf16[1,8,512,256]{3,1,2,0:T(8,128)(2,1)}, u32[]{:S(2)}) copy-start(bf16[1,8,512,256]{3,1,2,0:T(8,128)(2,1)} %copy-done.1) | copy-start | bytes 6291460
  117.6 35.1 %copy-start.16 = (bf16[3,3,256,256,1]{3,2,1,4,0:T(8,128)(2,1)S(1)}, bf16[3,3,256,256,1]{3,2,1,4,0:T(8,128)(2,1)}, u32[]{:S(2)}) copy-start(bf16[3,3,256,256,1]{3,2,1,4,0:T(8,128)(2,1)} %multiply_convert_fusion.2) | copy-start | bytes 3538948
  159.7 11.4 %collective-permute-start.6 = (bf16[1,1,512,256]{3,1,2,0:T(2,128)(2,1)}, bf16[1,1,512,256]{3,1,2,0:T(2,128)(2,1)}, u32[]{:S(2)}, u32[]{:S(2)}) collective-permute-start(bf16[1,1,512,256]{3,1,2,0:T(2,128)(2,1)} %slice.77), channel_id=1, source_target_pairs={{1,0},{2,1},{3,2},{4,3},{5,4},{6,5},{7,6},{8,7},{9,8},{10,9},{11,1... | collective-permute-start | bytes 786440 | tf_op jit(solution)/shard_map/ppermute | solution.py:18
  163.0 7.7 %collective-permute-start.5 = (bf16[1,1,512,256]{3,2,1,0:T(8,128)(2,1)S(1)}, bf16[1,1,512,256]{3,2,1,0:T(8,128)(2,1)S(1)}, u32[]{:S(2)}, u32[]{:S(2)}) collective-permute-start(bf16[1,1,512,256]{3,2,1,0:T(8,128)(2,1)S(1)} %slice.74), channel_id=1, source_target_pairs={{0,1},{1,2},{2,3},{3,4},{4,5},{5,6},{6,7},{7,8},{8,9},{9,10},{10,1... | collective-permute-start | bytes 786440 | tf_op jit(solution)/shard_map/ppermute | solution.py:17
  175.6 1.3 copy-start.15
  175.6 1.3 copy-start.19
  182.4 1.6 copy-start.6
  182.4 1.6 copy-start.12
  187.2 46.7 %copy-start.13 = (f32[1,2,144,256]{3,2,1,0:T(8,128)S(1)}, f32[1,2,144,256]{3,2,1,0:T(8,128)}, u32[]{:S(2)}) copy-start(f32[1,2,144,256]{3,2,1,0:T(8,128)} %param.12) | copy-start | bytes 884740
  187.2 46.7 %copy-start.17 = (f32[1,2,144,256]{3,2,1,0:T(8,128)S(1)}, f32[1,2,144,256]{3,2,1,0:T(8,128)}, u32[]{:S(2)}) copy-start(f32[1,2,144,256]{3,2,1,0:T(8,128)} %param.13) | copy-start | bytes 884740
  234.9 7.1 %collective-permute-start.2 = (bf16[2,1,2,144,256]{4,3,2,1,0:T(8,128)(2,1)S(1)}, bf16[2,1,2,144,256]{4,3,2,1,0:T(8,128)(2,1)S(1)}, u32[]{:S(2)}, u32[]{:S(2)}) collective-permute-start(bf16[2,1,2,144,256]{4,3,2,1,0:T(8,128)(2,1)S(1)} %param.2), channel_id=1, source_target_pairs={{0,64},{16,80},{32,96},{48,112},{64,0},{80,16},{96,32},{112,48},{1... | collective-permute-start | bytes 884744 | tf_op jit(solution)/shard_map/cond/branch_2_fun/ppermute | solution.py:33
Sparse Core Ops, SparseCore 0:
  11.1 54.9 all-gather.1
  154.5 79.3 reduce-scatter.1
where the time goes:
time: 255 us; the launch traced here: 250 us
  matrix products  67.2 us (26%)
  waiting for transfers between devices  65.6 us (26%)
  local copies, waits for them, and re-layouts  52.6 us (21%)
  other arithmetic  25.6 us (10%)
  starting transfers between devices  23.4 us (9%)
  between operations  15.5 us (6%)
    reduce_scatter x1, waiting for transfers between devices, shards(): lax.psum_scatter(jnp.stack([grad_first_full, grad_second_full])[None].ast...  44.9 us
    conv_general_dilated x2, matrix products, kernel_grad(): lax.conv_general_dilated(extended[None], upstream[None], (1, 1), ((0, 0),...  44.8 us
    ppermute x3, starting transfers between devices, extended_2(): before = lax.ppermute(last, axis, up)  15.7 us
    conv_general_dilated x2, matrix products, conv_behind(): lax.conv_general_dilated(extended[None], taps, (1, 1), ((0, 0), (1, 1)),...  15.2 us
    slice x7, local copies, waits for them, and re-layouts, shards(): preact = conv_ahead(paired[0], kernel_first)  13.1 us
    concatenate x2, other arithmetic, extended_2(): shard = jnp.concatenate([before, shard, after], axis=dim)  10.1 us
    unnamed x47, local copies, waits for them, and re-layouts  9.82 us
    ppermute x3, waiting for transfers between devices, extended_2(): before = lax.ppermute(last, axis, up)  9.35 us
  transfers between devices with their start and end apart: 9, of which 5 were waited for; matrix products, arithmetic and copies ran while one was open for 37% of the time, Pallas kernels for 0%

commit v1 on v0

--- a/solution.py
+++ b/solution.py
@@ -71,6 +71,19 @@
     return grad.reshape(-1, grad.shape[-1])
 
 
+def kernel_grad_behind(extended_upstream, field):
+    grad = lax.conv_general_dilated(
+        extended_upstream[None],
+        field[None],
+        (1, 1),
+        ((0, 0), (1, 1)),
+        dimension_numbers=("CHWN", "IHWO", "HWCN"),
+        preferred_element_type=jnp.float32,
+    )
+    grad = jnp.flip(grad, (0, 1))
+    return grad.reshape(-1, grad.shape[-1])
+
+
 def silu_slope(preact):
     sigma = jax.nn.sigmoid(preact)
     return sigma * (1.0 + preact * (1.0 - sigma))
@@ -96,33 +109,37 @@
     return 0.5 * (stacked + received)
 
 
+def gathered(weights, which):
+    return lax.all_gather(weights[0, which].astype(jnp.bfloat16), "space", axis=0, tiled=True)
+
+
+def scattered(grad):
+    return lax.psum_scatter(
+        grad.astype(jnp.bfloat16), "space", scatter_dimension=0, tiled=True
+    ).astype(jnp.float32)
+
+
 def shards(inputs, cotangent, land_mask, weights, momentum, step):
     row_count = inputs.shape[1]
     col_count = inputs.shape[2]
     space_count = lax.axis_size("space")
+    scale = 1.0 / math.sqrt(row_count * space_count * col_count)
     masked = cotangent[0] * land_mask.astype(jnp.bfloat16)[:, :, None]
-    kernels = lax.all_gather(weights.astype(jnp.bfloat16), "space", axis=2, tiled=True)
-    kernel_first = kernels[0, 0]
-    kernel_second = kernels[0, 1]
+    kernel_first = gathered(weights, 0)
+    kernel_second = gathered(weights, 1)
     paired = rim(jnp.stack([inputs[0], masked]))
-    preact = conv_ahead(paired[0], kernel_first)
+    input_ext = paired[0]
+    masked_ext = paired[1]
+    preact = conv_ahead(input_ext, kernel_first)
     hidden = jax.nn.silu(preact).astype(jnp.bfloat16)
-    hidden_ext = rim(hidden[None])[0]
-    back_mid = (conv_behind(paired[1], kernel_second) * silu_slope(preact)).astype(jnp.bfloat16)
+    share_second = scattered(kernel_grad_behind(masked_ext, hidden) * scale)
+    back_mid = (conv_behind(masked_ext, kernel_second) * silu_slope(preact)).astype(jnp.bfloat16)
+    share_first = scattered(kernel_grad(input_ext, back_mid) * scale)
     back_ext = rim(back_mid[None])[0]
-    input_ext = paired[0]
     grad_input = (conv_behind(back_ext, kernel_first) + masked.astype(jnp.float32)).astype(
         jnp.bfloat16
     )[None]
-    scale = 1.0 / math.sqrt(row_count * space_count * col_count)
-    grad_second_full = kernel_grad(hidden_ext, masked) * scale
-    grad_first_full = kernel_grad(input_ext, back_mid) * scale
-    shares = lax.psum_scatter(
-        jnp.stack([grad_first_full, grad_second_full])[None].astype(jnp.bfloat16),
-        "space",
-        scatter_dimension=2,
-        tiled=True,
-    ).astype(jnp.float32)
+    shares = jnp.stack([share_first, share_second])[None]
     moment = 0.9 * momentum + shares
     updated = weights - 0.01 * moment
     mixed = gossip(step, jnp.stack([updated, moment]), send_both)

time: 255 us -> 304 us (1.19)
  waiting for transfers between devices: 65.6 us -> 125 us
  local copies, waits for them, and re-layouts: 52.6 us -> 72.2 us
  matrix products: 67.2 us -> 48.1 us
  starting transfers between devices: 23.4 us -> 11 us
    reduce_scatter x1 -> x2, waiting for transfers between devices: 44.9 us -> 107 us  [scattered(): lax.psum_scatter(grad.astype(jnp.bfloat16), 'space', scatter_dimension=0,...]
    conv_general_dilated x2 -> x1, matrix products: 44.8 us -> 11.7 us  [kernel_grad(): lax.conv_general_dilated(extended[None], upstream[None], (1, 1), ((0, 0),...]
    slice x10 -> x16, local copies, waits for them, and re-layouts: 18.8 us -> 33.3 us  [the longest x7 18.6 us: shards(): input_ext = paired[0]]
    conv_general_dilated x0 -> x1, matrix products: none -> 13.3 us  [kernel_grad_behind(): lax.conv_general_dilated(extended_upstream[None], field[None], (1, 1), ((...]
    ppermute x3 -> x2, starting transfers between devices: 15.7 us -> 4.56 us  [extended_2(): before = lax.ppermute(last, axis, up)]
    unnamed x47 -> x48, local copies, waits for them, and re-layouts: 9.82 us -> 17.1 us
    ppermute x3 -> x2, waiting for transfers between devices: 9.35 us -> 4.21 us  [extended_2(): before = lax.ppermute(last, axis, up)]
    convert_element_type x19 -> x10, local copies, waits for them, and re-layouts: 11.2 us -> 6.35 us  [the longest x9 4.37 us: shards(): (conv_behind(masked_ext, kernel_second) * silu_slope(preact)).astype(jnp....]
  transfers between devices with their start and end apart: 9 -> 9, of which waited for: 5 -> 6; matrix products, arithmetic and copies ran while one was open for 37% -> 43% of each run, Pallas kernels for 0% -> 0%
where the time goes in v1:
time: 304 us; the launch traced here: 298 us
  waiting for transfers between devices  125 us (41%)
  local copies, waits for them, and re-layouts  72.2 us (24%)
  matrix products  48.1 us (16%)
  other arithmetic  26.2 us (9%)
  between operations  15.1 us (5%)
  starting transfers between devices  11 us (4%)
    reduce_scatter x2, waiting for transfers between devices, scattered(): lax.psum_scatter(grad.astype(jnp.bfloat16), 'space', scatter_dimension=0,...  107 us
    slice x7, local copies, waits for them, and re-layouts, shards(): input_ext = paired[0]  18.6 us
    unnamed x48, local copies, waits for them, and re-layouts  17.1 us
    conv_general_dilated x2, matrix products, conv_behind(): lax.conv_general_dilated(extended[None], taps, (1, 1), ((0, 0), (1, 1)),...  15.1 us
    slice x8, local copies, waits for them, and re-layouts, shards(): masked_ext = paired[1]  14 us
    conv_general_dilated x1, matrix products, kernel_grad_behind(): lax.conv_general_dilated(extended_upstream[None], field[None], (1, 1), ((...  13.3 us
    conv_general_dilated x1, matrix products, kernel_grad(): lax.conv_general_dilated(extended[None], upstream[None], (1, 1), ((0, 0),...  11.7 us
    concatenate x2, other arithmetic, extended_2(): shard = jnp.concatenate([before, shard, after], axis=dim)  10.1 us
  transfers between devices with their start and end apart: 9, of which 6 were waited for; matrix products, arithmetic and copies ran while one was open for 43% of the time, Pallas kernels for 0%

profile of v1, /device:TPU:2, one launch (start us, length us, event | category | flops | bytes accessed | tf_op | source)
XLA Modules:
  0.0 298.1 jit_solution(337054141233725164)
XLA Ops:
  9.8 2.9 copy.51
  12.8 3.1 %copy_multiply_fusion = bf16[1,8,512,256]{3,1,2,0:T(8,128)(2,1)S(1)} fusion(bf16[1,8,512,256]{3,2,1,0:T(8,128)(2,1)S(1)} %copy-done.9, bf16[8,512]{0,1:T(8,128)(2,1)S(1)} %copy.49), kind=kLoop, calls=%fused_computation.69 | loop fusion | flops 1048576 | bytes 4202496 | tf_op jit(solution)/shard_map/mul | solution.py:127
  20.3 2.4 collective-permute-start.3
  23.8 2.8 collective-permute-done.4
  27.4 4.2 %collective-permute-done.3 = bf16[2,1,512,256]{3,2,1,0:T(8,128)(2,1)} collective-permute-done((bf16[2,1,512,256]{3,2,1,0:T(8,128)(2,1)}, bf16[2,1,512,256]{3,2,1,0:T(8,128)(2,1)}, u32[]{:S(2)}, u32[]{:S(2)}) %collective-permute-start.3) | collective-permute-done | bytes 524320 | tf_op jit(solution)/shard_map/ppermute | solution.py:17
  33.5 6.1 %pad_maximum_fusion = bf16[2,10,512,256]{3,1,2,0:T(8,128)(2,1)S(1)} fusion(bf16[2,1,512,256]{3,1,2,0:T(2,128)(2,1)S(1)} %copy.55, bf16[1,8,512,256]{3,1,2,0:T(8,128)(2,1)S(1)} %copy-done.2, bf16[1,8,512,256]{3,1,2,0:T(8,128)(2,1)S(1)} %copy.51, bf16[2,1,512,256]{3,1,2,0:T(2,128)(2,1)S(1)} %copy.54), kind=kLoop, calls=%fused_computation | loop fusion | flops 20971520 | bytes 10485760 | tf_op jit(solution)/shard_map/concatenate | solution.py:19
  40.2 2.4 copy.104
  42.6 2.6 pad
  46.2 2.5 pad.2
  48.9 3.0 %reshape.57 = bf16[10,1,8,65,256]{4,3,2,0,1:T(8,128)(2,1)} reshape(bf16[10,1,520,256]{3,2,0,1:T(8,128)(2,1)S(1)} %pad.7.clone) | data formatting | bytes 5324800 | tf_op jit(solution)/shard_map/slice | solution.py:131
  51.9 3.0 %reshape.62 = bf16[10,8,65,256,1]{3,2,1,0,4:T(8,128)(2,1)} reshape(bf16[10,1,520,256]{3,2,0,1:T(8,128)(2,1)S(1)} %pad.7.clone) | data formatting | bytes 5324800 | tf_op jit(solution)/shard_map/slice | solution.py:131
  56.1 6.6 %fusion.91 = (bf16[10,1,8,64,256]{4,3,2,0,1:T(8,128)(2,1)}, bf16[10,1,8,64,256]{4,3,2,0,1:T(8,128)(2,1)}) fusion(bf16[10,1,8,65,256]{4,3,2,0,1:T(8,128)(2,1)} %reshape.57), kind=kLoop, calls=%fused_computation.101 | loop fusion | bytes 10485760 | tf_op jit(solution)/shard_map/slice | solution.py:131
  62.9 3.0 %reshape.41 = bf16[10,1,8,65,256]{4,3,2,0,1:T(8,128)(2,1)} reshape(bf16[10,1,520,256]{3,2,0,1:T(8,128)(2,1)S(1)} %pad.4.clone) | data formatting | bytes 5324800 | tf_op jit(solution)/shard_map/slice | solution.py:132
  65.9 3.5 %reshape.46 = bf16[10,8,65,256,1]{3,2,1,0,4:T(8,128)(2,1)} reshape(bf16[10,1,520,256]{3,2,0,1:T(8,128)(2,1)S(1)} %pad.4.clone) | data formatting | bytes 5324800 | tf_op jit(solution)/shard_map/slice | solution.py:132
  69.4 3.1 %copy.58 = bf16[10,1,8,65,256]{4,2,3,0,1:T(8,128)(2,1)S(1)} copy(bf16[10,1,8,65,256]{4,0,3,2,1:T(8,128)(2,1)} %bitcast.97) | data formatting | bytes 5324800 | tf_op jit(solution)/shard_map/conv_general_dilated | solution.py:52
  74.0 3.3 %copy.61 = bf16[10,1,8,65,256]{4,2,3,0,1:T(8,128)(2,1)S(1)} copy(bf16[10,1,8,65,256]{4,0,3,2,1:T(8,128)(2,1)} %bitcast.98) | data formatting | bytes 5324800 | tf_op jit(solution)/shard_map/conv_general_dilated | solution.py:39
  90.8 2.6 fusion.43
  93.5 2.6 fusion.45
  96.0 8.0 %fusion.27 = f32[8,8,65,256]{3,1,2,0:T(8,128)} fusion(bf16[3,3,256,256]{3,2,1,0:T(8,128)(2,1)} %bitcast.106, bf16[10,1,7,2,256]{4,2,3,0,1:T(8,128)(2,1)S(1)} %slice.63, bf16[10,1,8,65,256]{4,2,3,0,1:T(8,128)(2,1)S(1)} %copy.61), kind=kOutput, calls=%fused_computation.37 | convolution fusion | flops 4915568640 | bytes 8173568 | tf_op jit(solution)/shard_map/conv_general_dilated | solution.py:39
  104.0 4.8 %all-gather.5.cloned.1.call-done = bf16[1,1,2304,256]{3,2,1,0:T(8,128)(2,1)} async-done(((bf16[1,1,144,256]{3,2,1,0:T(8,128)(2,1)}), bf16[1,1,2304,256]{3,2,1,0:T(8,128)(2,1)}) %all-gather.5.cloned.1.call-update) | async-done | bytes 1179664 | tf_op jit(solution)/shard_map/all_gather | solution.py:113
  108.8 9.6 %multiply_convert_fusion = bf16[8,8,65,256]{3,1,2,0:T(8,128)(2,1)S(1)} fusion(f32[8,8,65,256]{3,1,2,0:T(8,128)} %fusion.27, bf16[3,3,256,256]{3,2,1,0:T(8,128)(2,1)} %bitcast.108, bf16[10,1,7,2,256]{4,2,3,0,1:T(8,128)(2,1)S(1)} %slice.60, bf16[10,1,8,65,256]{4,2,3,0,1:T(8,128)(2,1)} %copy-done.11, pred[8,65]{0,1:T(8,128)(4,1)S(1)} %copy-done.17), kind=kOutput, calls=%fused_computation.23 | convolution fusion | flops 4927283200 | bytes 10304008 | tf_op jit(solution)/shard_map/conv_general_dilated | solution.py:52
  121.1 2.2 collective-permute-start.5
  124.9 3.4 %collective-permute-start.6 = (bf16[1,1,512,256]{3,1,2,0:T(2,128)(2,1)}, bf16[1,1,512,256]{3,1,2,0:T(2,128)(2,1)}, u32[]{:S(2)}, u32[]{:S(2)}) collective-permute-start(bf16[1,1,512,256]{3,1,2,0:T(2,128)(2,1)} %slice.69), channel_id=1, source_target_pairs={{1,0},{2,1},{3,2},{4,3},{5,4},{6,5},{7,6},{8,7},{9,8},{10,9},{11,1... | collective-permute-start | bytes 786440 | tf_op jit(solution)/shard_map/ppermute | solution.py:18
  128.3 11.7 %multiply_convert_fusion.2 = bf16[3,3,256,256,1]{3,2,1,4,0:T(8,128)(2,1)} fusion(bf16[8,8,65,256]{3,1,2,0:T(8,128)(2,1)S(1)} %multiply_convert_fusion, pred[8,65]{0,1:T(8,128)(4,1)S(1)} %copy-done.17, bf16[10,8,65,256,1]{3,1,4,2,0:T(8,128)(2,1)} %get-tuple-element.45, bf16[10,8,65,256,1]{3,1,4,2,0:T(8,128)(2,1)} %copy.77, ...), kind=kOutput, calls=%fused_computation.58 | convolution fusion | flops 4917567488 | bytes 11297288 | tf_op jit(solution)/shard_map/conv_general_dilated | solution.py:63
  140.0 13.3 %fusion.65 = f32[3,3,256,256]{2,3,1,0:T(8,128)S(1)} fusion(f32[8,8,65,256]{3,1,2,0:T(8,128)} %fusion.27, pred[8,65]{0,1:T(8,128)(4,1)S(1)} %copy-done.17, bf16[10,8,65,256,1]{3,1,4,2,0:T(8,128)(2,1)} %get-tuple-element.43, bf16[10,8,65,256,1]{3,1,4,2,0:T(8,128)(2,1)} %copy.85, bf16[10,8,65,256,1]{3,1,4,2,0:T(8,128)(2,1)} %get-tuple-element.42), kind=kOutput, calls=%fused_computation.70 | convolution fusion | flops 4922777600 | bytes 14606856 | tf_op jit(solution)/shard_map/conv_general_dilated | solution.py:75
  157.1 3.9 %maximum_bitcast_fusion = bf16[10,1,512,256]{3,0,2,1:T(8,128)(2,1)S(1)} fusion(bf16[1,1,512,256]{3,1,2,0:T(2,128)(2,1)} %collective-permute-done.6, bf16[1,8,512,256]{3,1,2,0:T(8,128)(2,1)S(1)} %slice_bitcast_fusion.3, bf16[1,1,512,256]{3,1,2,0:T(2,128)(2,1)S(1)} %copy.66), kind=kLoop, calls=%fused_computation.31 | loop fusion | flops 7864320 | bytes 5242880 | tf_op jit(solution)/shard_map/concatenate | solution.py:19
  162.9 5.5 %broadcast_select_fusion = f32[8,8,65,256]{3,1,2,0:T(8,128)S(1)} fusion(pred[8,65]{0,1:T(8,128)(4,1)S(1)} %copy-done.17, bf16[3,3,256,256]{3,2,1,0:T(8,128)(2,1)S(1)} %bitcast.107, bf16[10,1,7,2,256]{4,2,3,0,1:T(8,128)(2,1)S(1)} %slice.70, bf16[10,1,8,65,256]{4,2,3,0,1:T(8,128)(2,1)S(1)} %copy.69), kind=kOutput, calls=%fused_computation.64 | convolution fusion | flops 4916633600 | bytes 8174088 | tf_op jit(solution)/shard_map/conv_general_dilated | solution.py:52
  170.0 3.3 %fusion.20 = bf16[1,8,512,256]{3,1,2,0:T(8,128)(2,1)S(1)} fusion(f32[8,1,520,256]{3,0,2,1:T(8,128)S(1)} %bitcast.100, bf16[8,512]{0,1:T(8,128)(2,1)S(1)} %copy-done.13, bf16[1,8,512,256]{3,2,1,0:T(8,128)(2,1)S(1)} %copy-done.10), kind=kLoop, calls=%fused_computation.28 | loop fusion | flops 4194304 | bytes 8396800 | tf_op jit(solution)/shard_map/convert_element_type | solution.py:139
  175.0 36.7 %reduce-scatter.3.cloned.1.call-done = bf16[144,256]{1,0:T(8,128)(2,1)} async-done(((bf16[2304,256]{1,0:T(8,128)(2,1)}), bf16[144,256]{1,0:T(8,128)(2,1)}) %reduce-scatter.3.cloned.1.call-update) | async-done | bytes 73744 | tf_op jit(solution)/shard_map/reduce_scatter | solution.py:117
  211.7 70.5 %reduce-scatter.5.cloned.1.call-done = bf16[144,256]{1,0:T(8,128)(2,1)} async-done(((bf16[2304,256]{1,0:T(8,128)(2,1)}), bf16[144,256]{1,0:T(8,128)(2,1)}) %reduce-scatter.5.cloned.1.call-update) | async-done | bytes 73744 | tf_op jit(solution)/shard_map/reduce_scatter | solution.py:117
  283.2 7.3 %conditional.4 = (f32[2,1,2,144,256]{4,3,2,1,0:T(8,128)S(1)}) conditional(s32[]{:T(128)} %clamp.3, bf16[2,1,2,144,256]{4,3,2,1,0:T(8,128)(2,1)S(1)} %pad_maximum_fusion.3, bf16[2,1,2,144,256]{4,3,2,1,0:T(8,128)(2,1)S(1)} %pad_maximum_fusion.3, bf16[2,1,2,144,256]{4,3,2,1,0:T(8,128)(2,1)S(1)} %pad_maximum_fusion.3), branch_computations={%region_2.3_spmd, %region_3.4_spmd, %region_4.5_spmd} | conditional | flops 147456 | bytes 2064432
  284.0 6.4 %collective-permute-done.2 = bf16[2,1,2,144,256]{4,3,2,1,0:T(8,128)(2,1)S(1)} collective-permute-done((bf16[2,1,2,144,256]{4,3,2,1,0:T(8,128)(2,1)S(1)}, bf16[2,1,2,144,256]{4,3,2,1,0:T(8,128)(2,1)S(1)}, u32[]{:S(2)}, u32[]{:S(2)}) %collective-permute-start.2) | collective-permute-done | bytes 294944 | tf_op jit(solution)/shard_map/cond/branch_2_fun/ppermute | solution.py:33
  (99 shorter events, 43.9 us)
Async XLA Ops:
  7.2 88.9 %all-gather.7.cloned.1.call-start = ((), (), s32[]{:S(2)}) async-start(), calls=%async_computation.5 | async-start | bytes 1253376 | tf_op jit(solution)/shard_map/all_gather | solution.py:113
  8.9 100.0 %all-gather.5.cloned.1.call-start = ((), (), s32[]{:S(2)}) async-start(), calls=%async_computation.4 | async-start | bytes 1253376 | tf_op jit(solution)/shard_map/all_gather | solution.py:113
  9.8 6.0 %copy-start.12 = (bf16[8,512]{0,1:T(8,128)(2,1)}, bf16[8,512]{0,1:T(8,128)(2,1)S(1)}, u32[]{:S(2)}) copy-start(bf16[8,512]{0,1:T(8,128)(2,1)S(1)} %copy.49) | copy-start | bytes 24580
  9.8 2.9 copy-start.9
  15.9 1.6 copy-start.1
  17.5 9.1 %collective-permute-start.4 = (bf16[2,1,512,256]{3,2,1,0:T(8,128)(2,1)S(1)}, bf16[2,1,512,256]{3,2,1,0:T(8,128)(2,1)S(1)}, u32[]{:S(2)}, u32[]{:S(2)}) collective-permute-start(bf16[2,1,512,256]{3,2,1,0:T(8,128)(2,1)S(1)} %copy.53), channel_id=1, source_target_pairs={{1,0},{2,1},{3,2},{4,3},{5,4},{6,5},{7,6},{8,7},{9,8},{10,9},{11,1... | collective-permute-start | bytes 1572872 | tf_op jit(solution)/shard_map/ppermute | solution.py:18
  20.3 11.2 %collective-permute-start.3 = (bf16[2,1,512,256]{3,2,1,0:T(8,128)(2,1)}, bf16[2,1,512,256]{3,2,1,0:T(8,128)(2,1)}, u32[]{:S(2)}, u32[]{:S(2)}) collective-permute-start(bf16[2,1,512,256]{3,2,1,0:T(8,128)(2,1)} %copy.52), channel_id=1, source_target_pairs={{0,1},{1,2},{2,3},{3,4},{4,5},{5,6},{6,7},{7,8},{8,9},{9,10},{10,1... | collective-permute-start | bytes 1572872 | tf_op jit(solution)/shard_map/ppermute | solution.py:17
  22.8 188.9 %reduce-scatter.3.cloned.1.call-start = ((), (), s32[]{:S(2)}) async-start(), calls=%async_computation.2 | async-start | bytes 1253376 | tf_op jit(solution)/shard_map/reduce_scatter | solution.py:117
  23.8 9.7 %copy-start.2 = (bf16[1,8,512,256]{3,1,2,0:T(8,128)(2,1)S(1)}, bf16[1,8,512,256]{3,1,2,0:T(8,128)(2,1)}, u32[]{:S(2)}) copy-start(bf16[1,8,512,256]{3,1,2,0:T(8,128)(2,1)} %copy-done.1) | copy-start | bytes 6291460
  56.1 6.7 %copy-start.7 = (bf16[10,1,512,256]{3,2,0,1:T(8,128)(2,1)S(1)}, bf16[10,1,512,256]{3,2,0,1:T(8,128)(2,1)}, u32[]{:S(2)}) copy-start(bf16[10,1,512,256]{3,2,0,1:T(8,128)(2,1)} %copy.104) | copy-start | bytes 7864324
  72.5 1.5 copy-start.11
  74.0 3.3 %copy-start.4 = (bf16[10,8,65,256,1]{3,2,1,0,4:T(8,128)(2,1)S(1)}, bf16[10,8,65,256,1]{3,2,1,0,4:T(8,128)(2,1)}, u32[]{:S(2)}) copy-start(bf16[10,8,65,256,1]{3,2,1,0,4:T(8,128)(2,1)} %reshape.62) | copy-start | bytes 7987204
  77.4 2.2 copy-start.6
  79.5 1.8 copy-start.5
  79.6 3.6 %copy-start.3 = (bf16[10,8,65,256,1]{3,2,1,0,4:T(8,128)(2,1)S(1)}, bf16[10,8,65,256,1]{3,2,1,0,4:T(8,128)(2,1)}, u32[]{:S(2)}) copy-start(bf16[10,8,65,256,1]{3,2,1,0,4:T(8,128)(2,1)} %reshape.46) | copy-start | bytes 7987204
  81.3 1.8 copy-start
  96.0 12.8 %copy-start.17 = (pred[8,65]{0,1:T(8,128)(4,1)S(1)}, pred[8,65]{0,1:T(8,128)(4,1)}, u32[]{:S(2)}) copy-start(pred[8,65]{0,1:T(8,128)(4,1)} %constant.54) | copy-start | bytes 1564
  121.1 34.6 %collective-permute-start.5 = (bf16[1,1,512,256]{3,2,1,0:T(8,128)(2,1)}, bf16[1,1,512,256]{3,2,1,0:T(8,128)(2,1)}, u32[]{:S(2)}, u32[]{:S(2)}) collective-permute-start(bf16[1,1,512,256]{3,2,1,0:T(8,128)(2,1)} %slice.66), channel_id=1, source_target_pairs={{0,1},{1,2},{2,3},{3,4},{4,5},{5,6},{6,7},{7,8},{8,9},{9,10},{10,1... | collective-permute-start | bytes 786440 | tf_op jit(solution)/shard_map/ppermute | solution.py:17
  124.9 32.2 %collective-permute-start.6 = (bf16[1,1,512,256]{3,1,2,0:T(2,128)(2,1)}, bf16[1,1,512,256]{3,1,2,0:T(2,128)(2,1)}, u32[]{:S(2)}, u32[]{:S(2)}) collective-permute-start(bf16[1,1,512,256]{3,1,2,0:T(2,128)(2,1)} %slice.69), channel_id=1, source_target_pairs={{1,0},{2,1},{3,2},{4,3},{5,4},{6,5},{7,6},{8,7},{9,8},{10,9},{11,1... | collective-permute-start | bytes 786440 | tf_op jit(solution)/shard_map/ppermute | solution.py:18
  140.0 142.2 %reduce-scatter.5.cloned.1.call-start = ((), (), s32[]{:S(2)}) async-start(), calls=%async_computation.3 | async-start | bytes 1253376 | tf_op jit(solution)/shard_map/reduce_scatter | solution.py:117
  153.3 2.3 copy-start.8
  161.6 1.3 copy-start.16
  168.4 1.6 copy-start.10
  168.4 1.6 copy-start.13
  173.3 108.9 %copy-start.14 = (f32[1,2,144,256]{3,2,1,0:T(8,128)S(1)}, f32[1,2,144,256]{3,2,1,0:T(8,128)}, u32[]{:S(2)}) copy-start(f32[1,2,144,256]{3,2,1,0:T(8,128)} %param.12) | copy-start | bytes 884740
  173.3 108.9 %copy-start.15 = (f32[1,2,144,256]{3,2,1,0:T(8,128)S(1)}, f32[1,2,144,256]{3,2,1,0:T(8,128)}, u32[]{:S(2)}) copy-start(f32[1,2,144,256]{3,2,1,0:T(8,128)} %param.13) | copy-start | bytes 884740
  283.3 7.2 %collective-permute-start.2 = (bf16[2,1,2,144,256]{4,3,2,1,0:T(8,128)(2,1)S(1)}, bf16[2,1,2,144,256]{4,3,2,1,0:T(8,128)(2,1)S(1)}, u32[]{:S(2)}, u32[]{:S(2)}) collective-permute-start(bf16[2,1,2,144,256]{4,3,2,1,0:T(8,128)(2,1)S(1)} %param.2), channel_id=1, source_target_pairs={{0,64},{16,80},{32,96},{48,112},{64,0},{80,16},{96,32},{112,48},{1... | collective-permute-start | bytes 884744 | tf_op jit(solution)/shard_map/cond/branch_2_fun/ppermute | solution.py:33
Sparse Core Ops, SparseCore 0:
  10.4 51.1 all-gather.6
  64.6 44.1 all-gather.4
  140.1 71.5 reduce-scatter.2
  215.9 66.2 reduce-scatter.4
